TPU v7x, 32 devices: a whole 2x2x4 slice. The times are simulated.
32 devices in a mesh: groups: 2 (over y), tm: 16 (over z, x, core).
Axes of the slice: x: 2, y: 2, z: 4, core: 2. Of those that a mesh axis runs over, the one named last changes fastest.
Arguments:
- noisy: bfloat16 [256, 16, 16, 256], P(('groups', 'tm')), parts along dimension 0, may hold values from -6 to 6
- observed: float32 [256, 16, 256], P(('groups', 'tm')), parts along dimension 0, may hold values from -6 to 6
- obs_mask: int32 [256, 16, 256], P(('groups', 'tm')), parts along dimension 0, may hold values 0 or 1
- obs_channel: int32 [256, 16, 256], P(('groups', 'tm')), parts along dimension 0, may hold values from 0 to 15
- step_index: int32 [2], P('groups'), parts along dimension 0, may hold values from 0 to 63
- w_first: bfloat16 [128, 80, 3, 3], replicated, may hold values from -0.21875 to 0.21875
- b_first: float32 [128], replicated, may hold values from -3 to 3
- w_second: bfloat16 [16, 128, 3, 3], replicated, may hold values from -0.1875 to 0.1875
- b_second: float32 [16], replicated, may hold values from -3 to 3
Outputs:
- guided: float32 [256, 16, 16, 256], P(('groups', 'tm')), parts along dimension 0
There are 2 independent parts, one for each index of `groups`. A program takes and returns all parts, laid end to end along the dimension named above; an argument that names none is the same for every part. Nothing has to cross between parts.
All inputs are finite; a program needn't handle non-finite values. No bound on the sum of `obs_mask` on one device may be relied on, other than what follows from the above.
Results may differ from a plain program's by a relative error of at most 0.0015.
Values may be sent and summed in bfloat16 or wider, within the bound.
No kernel may reach another device: no remote copies, remote signals or barrier semaphores. Data moves between devices by JAX's collectives and lax.ppermute only.
A program may use at most 128 MiB of HBM per device.

v0:
```python
import jax
import jax.numpy as jnp
from jax import lax
from jax.sharding import PartitionSpec as P

STEPS = 64
ROWS = 16
COLS = 256


sigma_low = 0.1
sigma_ratio = 20.0


def with_halo(x, sides, width):
    for axis, dim in sides:
        peers, length = (lax.axis_size(axis), x.shape[dim])
        up = [(i, (i + 1) % peers) for i in range(peers - 1)]
        down = [(j, i) for i, j in up]
        last = lax.slice_in_dim(x, length - width, length, axis=dim)
        initial = lax.slice_in_dim(x, 0, width, axis=dim)
        before = lax.ppermute(last, axis, up)
        after = lax.ppermute(initial, axis, down)
        x = jnp.concatenate([before, x, after], axis=dim)
    return x


def passed_along(value, axis, steps):
    count = lax.axis_size(axis)
    initial, last = (max(0, -steps), min(count, count - steps))
    return lax.ppermute(value, axis, [(source, source + steps) for source in range(initial, last)])


def conv(value, kernel):
    return lax.conv_general_dilated(
        value,
        kernel,
        (1, 1),
        ((1, 1), (1, 1)),
        dimension_numbers=("NCHW", "OIHW", "NCHW"),
        preferred_element_type=jnp.float32,
    )


def conv_back(grad, kernel):
    flipped = jnp.transpose(kernel, (1, 0, 2, 3))[:, :, ::-1, ::-1]
    return conv(grad, flipped)


def stack_windows(source, frames, span):
    return jnp.concatenate([source[k : k + frames] for k in range(span)], axis=1)


def per_device(
    noisy, observed, obs_mask, obs_channel, step_index, w_first, b_first, w_second, b_second
):
    frames = noisy.shape[0]
    chans = noisy.shape[1]
    span = w_first.shape[1] // chans
    level = step_index[0].astype(jnp.float32) / jnp.float32(STEPS - 1)
    sigma = jnp.float32(sigma_low) * jnp.exp(jnp.log(jnp.float32(sigma_ratio)) * level)
    c_in = 1.0 / jnp.sqrt(1.0 + sigma * sigma)
    weight_obs = 1.0 / (1.0 + sigma * sigma)
    scaled = (c_in * noisy.astype(jnp.float32)).astype(jnp.bfloat16)
    extended = with_halo(scaled, (("tm", 0),), 2)
    pre = conv(stack_windows(extended, frames, span), w_first)
    pre = pre + b_first[None, :, None, None]
    hidden = jax.nn.silu(pre).astype(jnp.bfloat16)
    den = noisy.astype(jnp.float32) + conv(hidden, w_second) + b_second[None, :, None, None]
    channel_ids = jnp.arange(chans, dtype=jnp.int32)
    select = (
        (obs_channel[:, None, :, :] == channel_ids[None, :, None, None])
        & (obs_mask[:, None, :, :] == 1)
    ).astype(jnp.float32)
    misfit = select * (den - observed[:, None, :, :])
    misfit_b = misfit.astype(jnp.bfloat16)
    sig = jax.nn.sigmoid(pre)
    grad_hidden = (conv_back(misfit_b, w_second) * (sig * (1.0 + pre * (1.0 - sig)))).astype(
        jnp.bfloat16
    )
    grad_window = conv_back(grad_hidden, w_first).reshape(frames, span, chans, ROWS, COLS)
    back_pad = jnp.zeros((frames + 4, chans, ROWS, COLS), jnp.float32)
    for k in range(span):
        back_pad = back_pad.at[k : k + frames].add(grad_window[:, k])
    from_right = passed_along(back_pad[:2].astype(jnp.bfloat16), "tm", -1).astype(jnp.float32)
    from_left = passed_along(back_pad[frames + 2 :].astype(jnp.bfloat16), "tm", 1).astype(
        jnp.float32
    )
    back = back_pad[2 : frames + 2]
    back = back.at[frames - 2 :].add(from_right)
    back = back.at[:2].add(from_left)
    return den - weight_obs * (misfit + c_in * back)


def solution(mesh):
    return jax.shard_map(
        per_device,
        mesh=mesh,
        in_specs=(
            P(("groups", "tm"), None, None, None),
            P(("groups", "tm"), None, None),
            P(("groups", "tm"), None, None),
            P(("groups", "tm"), None, None),
            P("groups"),
            P(),
            P(),
            P(),
            P(),
        ),
        out_specs=P(("groups", "tm"), None, None, None),
        check_vma=False,
    )
```

profile of v0, /device:TPU:1, one launch (start us, length us, event | category | flops | bytes accessed | tf_op | source)
XLA Modules:
  0.0 169.3 jit_solution(11622179099909798081)
XLA Ops:
  0.8 1.4 fusion.1
  2.3 4.6 %collective-permute-start = (bf16[2,16,16,256]{3,2,1,0:T(8,128)(2,1)S(1)}, bf16[2,16,16,256]{3,2,1,0:T(8,128)(2,1)S(1)}, u32[]{:S(2)}, u32[]{:S(2)}) collective-permute-start(bf16[2,16,16,256]{3,2,1,0:T(8,128)(2,1)S(1)} %get-tuple-element.90), channel_id=1, source_target_pairs={{0,1},{1,2},{2,3},{3,4},{4,5},{5,6},{6,7},{7,8},{8,9},{9,10},{10,1... | collective-permute-start | bytes 786440 | tf_op jit(solution)/shard_map/ppermute | solution.py:22
  6.9 1.9 %collective-permute-start.1 = (bf16[2,16,16,256]{3,2,1,0:T(8,128)(2,1)S(1)}, bf16[2,16,16,256]{3,2,1,0:T(8,128)(2,1)S(1)}, u32[]{:S(2)}, u32[]{:S(2)}) collective-permute-start(bf16[2,16,16,256]{3,2,1,0:T(8,128)(2,1)S(1)} %get-tuple-element.89), channel_id=1, source_target_pairs={{1,0},{2,1},{3,2},{4,3},{5,4},{6,5},{7,6},{8,7},{9,8},{10,9},{11,1... | collective-permute-start | bytes 786440 | tf_op jit(solution)/shard_map/ppermute | solution.py:23
  8.9 1.3 collective-permute-done
  11.3 1.1 fusion.17
  12.4 1.2 constant_dynamic-update-slice_fusion
  16.8 9.0 %copy.51 = bf16[8,80,16,256]{1,0,3,2:T(8,128)(2,1)} copy(bf16[8,80,16,256]{3,2,1,0:T(8,128)(2,1)} %fusion.16) | data formatting | bytes 10485760 | tf_op jit(solution)/shard_map/concatenate | solution.py:51
  25.8 23.8 %fusion.22 = f32[8,128,16,256]{1,0,3,2:T(8,128)S(1)} fusion(bf16[8,80,16,256]{1,0,3,2:T(8,128)(2,1)} %copy.51, bf16[128,80,3,3]{0,1,3,2:T(8,128)(2,1)S(1)} %copy-done), kind=kOutput, calls=%fused_computation.48 | convolution fusion | flops 5773066240 | bytes 22204416 | tf_op jit(solution)/shard_map/conv_general_dilated | solution.py:35
  49.6 5.7 %copy-done.9 = f32[8,128,16,256]{1,0,3,2:T(8,128)} copy-done((f32[8,128,16,256]{1,0,3,2:T(8,128)}, f32[8,128,16,256]{1,0,3,2:T(8,128)S(1)}, u32[]{:S(2)}) %copy-start.9) | copy-done | bytes 16777240
  55.3 22.4 %fusion = f32[8,16,16,256]{1,0,3,2:T(8,128)} fusion(bf16[16,128,3,3]{1,0,3,2:T(8,128)(2,1)S(1)} %copy-done.7, f32[8,128,16,256]{1,0,3,2:T(8,128)S(1)} %fusion.22, f32[128]{0:T(128)S(1)} %copy-done.8), kind=kOutput, calls=%fused_computation.3 | convolution fusion | flops 1179779072 | bytes 18911744 | tf_op jit(solution)/shard_map/conv_general_dilated | solution.py:35
  77.7 8.2 %copy.52 = f32[8,16,16,256]{3,2,1,0:T(8,128)S(1)} copy(f32[8,16,16,256]{1,0,3,2:T(8,128)} %fusion) | data formatting | bytes 4194304 | tf_op jit(solution)/shard_map/conv_general_dilated | solution.py:35
  86.0 2.6 %fusion.10 = bf16[8,16,16,256]{3,2,1,0:T(8,128)(2,1)} fusion(f32[8,16,16,256]{3,2,1,0:T(8,128)S(1)} %copy.52, bf16[8,16,16,256]{3,2,1,0:T(8,128)(2,1)S(1)} %copy-done.2, f32[8,16,256]{2,1,0:T(8,128)S(1)} %copy-done.3, s32[8,16,256]{2,1,0:T(8,128)} %param.26, f32[16]{0:T(128)S(1)} %copy-done.6, pred[8,16,256]{2,1,0:T(8,128)(4,1)S(1)} %broadcast_compare_fusion), kind=kLoop, calls=%fused_computation.22 | loop fusion | flops 4194304 | bytes 4489280 | tf_op jit(solution)/shard_map/convert_element_type | solution.py:76
  88.6 7.5 %copy.53 = bf16[8,16,16,256]{1,0,3,2:T(8,128)(2,1)} copy(bf16[8,16,16,256]{3,2,1,0:T(8,128)(2,1)} %fusion.10) | data formatting | bytes 2097152 | tf_op jit(solution)/shard_map/convert_element_type | solution.py:76
  96.1 16.5 %multiply_convert_fusion = bf16[8,128,16,256]{1,0,3,2:T(8,128)(2,1)S(1)} fusion(f32[8,128,16,256]{1,0,3,2:T(8,128)} %copy-done.9, bf16[8,16,16,256]{1,0,3,2:T(8,128)(2,1)} %copy.53, bf16[16,128,3,3]{1,0,3,2:T(8,128)(2,1)S(1)} %copy-done.7, f32[128]{0:T(128)S(1)} %copy-done.8), kind=kOutput, calls=%fused_computation | convolution fusion | flops 1196556288 | bytes 26251776 | tf_op jit(solution)/shard_map/conv_general_dilated | solution.py:35
  112.5 22.2 %fusion.23 = f32[8,80,16,256]{1,0,3,2:T(8,128)} fusion(bf16[8,128,16,256]{1,0,3,2:T(8,128)(2,1)S(1)} %multiply_convert_fusion, bf16[128,80,3,3]{0,1,3,2:T(8,128)(2,1)S(1)} %copy-done), kind=kOutput, calls=%fused_computation.49 | convolution fusion | flops 5773066240 | bytes 19058688 | tf_op jit(solution)/shard_map/conv_general_dilated | solution.py:35
  134.7 11.8 %copy.54 = f32[8,80,16,256]{3,2,1,0:T(8,128)} copy(f32[8,80,16,256]{1,0,3,2:T(8,128)} %fusion.23) | data formatting | bytes 20971520 | tf_op jit(solution)/shard_map/conv_general_dilated | solution.py:35
  146.5 1.8 %slice_bitcast_fusion.4 = f32[8,16,16,256]{3,2,1,0:T(8,128)S(1)} fusion(f32[8,5,16,16,256]{4,3,2,1,0:T(8,128)} %bitcast.44), kind=kLoop, calls=%fused_computation.19 | loop fusion | bytes 4194304 | tf_op jit(solution)/shard_map/add | solution.py:84
  148.7 2.3 %fusion.9 = f32[12,16,16,256]{3,2,1,0:T(8,128)S(1)} fusion(f32[12,16,16,256]{3,2,1,0:T(8,128)S(1)} %scatter-add.24, f32[8,5,16,16,256]{4,3,2,1,0:T(8,128)} %bitcast.45), kind=kLoop, calls=%fused_computation.18 | loop fusion | flops 524288 | bytes 6291456 | tf_op jit(solution)/shard_map/scatter-add | solution.py:84
  151.0 1.9 %copy-done.1 = f32[8,80,16,256]{3,2,1,0:T(8,128)S(1)} copy-done((f32[8,80,16,256]{3,2,1,0:T(8,128)S(1)}, f32[8,80,16,256]{3,2,1,0:T(8,128)}, u32[]{:S(2)}) %copy-start.1) | copy-done | bytes 10485784
  154.9 1.9 %collective-permute-start.2 = (bf16[2,16,16,256]{3,2,1,0:T(8,128)(2,1)S(1)}, bf16[2,16,16,256]{3,2,1,0:T(8,128)(2,1)S(1)}, u32[]{:S(2)}, u32[]{:S(2)}) collective-permute-start(bf16[2,16,16,256]{3,2,1,0:T(8,128)(2,1)S(1)} %slice.338), channel_id=1, source_target_pairs={{1,0},{2,1},{3,2},{4,3},{5,4},{6,5},{7,6},{8,7},{9,8},{10,9},{11,1... | collective-permute-start | bytes 786440 | tf_op jit(solution)/shard_map/ppermute | solution.py:31
  156.9 3.6 %collective-permute-start.3 = (bf16[2,16,16,256]{3,2,1,0:T(8,128)(2,1)S(1)}, bf16[2,16,16,256]{3,2,1,0:T(8,128)(2,1)S(1)}, u32[]{:S(2)}, u32[]{:S(2)}) collective-permute-start(bf16[2,16,16,256]{3,2,1,0:T(8,128)(2,1)S(1)} %slice.337), channel_id=1, source_target_pairs={{0,1},{1,2},{2,3},{3,4},{4,5},{5,6},{6,7},{7,8},{8,9},{9,10},{10,1... | collective-permute-start | bytes 786440 | tf_op jit(solution)/shard_map/ppermute | solution.py:31
  160.8 1.8 %collective-permute-done.2 = bf16[2,16,16,256]{3,2,1,0:T(8,128)(2,1)S(1)} collective-permute-done((bf16[2,16,16,256]{3,2,1,0:T(8,128)(2,1)S(1)}, bf16[2,16,16,256]{3,2,1,0:T(8,128)(2,1)S(1)}, u32[]{:S(2)}, u32[]{:S(2)}) %collective-permute-start.2) | collective-permute-done | bytes 262176 | tf_op jit(solution)/shard_map/ppermute | solution.py:31
  162.7 3.9 %collective-permute-done.3 = bf16[2,16,16,256]{3,2,1,0:T(8,128)(2,1)S(1)} collective-permute-done((bf16[2,16,16,256]{3,2,1,0:T(8,128)(2,1)S(1)}, bf16[2,16,16,256]{3,2,1,0:T(8,128)(2,1)S(1)}, u32[]{:S(2)}, u32[]{:S(2)}) %collective-permute-start.3) | collective-permute-done | bytes 262176 | tf_op jit(solution)/shard_map/ppermute | solution.py:31
  166.7 2.3 %multiply_subtract_fusion = f32[8,16,16,256]{3,2,1,0:T(8,128)} fusion(f32[8,16,16,256]{3,2,1,0:T(8,128)S(1)} %fusion.18, f32[8,16,16,256]{3,2,1,0:T(8,128)S(1)} %copy.52, bf16[8,16,16,256]{3,2,1,0:T(8,128)(2,1)S(1)} %copy-done.2, f32[8,16,256]{2,1,0:T(8,128)S(1)} %copy-done.3, s32[8,16,256]{2,1,0:T(8,128)S(1)} %copy-done.4, f32[]{:T(128)} %bitcast.1, ...), kind=kLoop, calls=%fused_computation.20 | loop fusion | flops 5767168 | bytes 7635016 | tf_op jit(solution)/shard_map/sub | solution.py:92
  (34 shorter events, 7.1 us)
Async XLA Ops:
  0.0 25.8 %copy-start = (bf16[128,80,3,3]{0,1,3,2:T(8,128)(2,1)S(1)}, bf16[128,80,3,3]{0,1,3,2:T(8,128)(2,1)}, u32[]{:S(2)}) copy-start(bf16[128,80,3,3]{0,1,3,2:T(8,128)(2,1)} %param.28) | copy-start | bytes 552964
  0.0 8.9 %copy-start.5 = (s32[8,16,256]{2,1,0:T(8,128)S(1)}, s32[8,16,256]{2,1,0:T(8,128)}, u32[]{:S(2)}) copy-start(s32[8,16,256]{2,1,0:T(8,128)} %param.25) | copy-start | bytes 393220
  2.2 10.2 %copy-start.2 = (bf16[8,16,16,256]{3,2,1,0:T(8,128)(2,1)S(1)}, bf16[8,16,16,256]{3,2,1,0:T(8,128)(2,1)}, u32[]{:S(2)}) copy-start(bf16[8,16,16,256]{3,2,1,0:T(8,128)(2,1)} %param.23) | copy-start | bytes 3145732
  2.3 7.9 %collective-permute-start = (bf16[2,16,16,256]{3,2,1,0:T(8,128)(2,1)S(1)}, bf16[2,16,16,256]{3,2,1,0:T(8,128)(2,1)S(1)}, u32[]{:S(2)}, u32[]{:S(2)}) collective-permute-start(bf16[2,16,16,256]{3,2,1,0:T(8,128)(2,1)S(1)} %get-tuple-element.90), channel_id=1, source_target_pairs={{0,1},{1,2},{2,3},{3,4},{4,5},{5,6},{6,7},{7,8},{8,9},{9,10},{10,1... | collective-permute-start | bytes 786440 | tf_op jit(solution)/shard_map/ppermute | solution.py:22
  6.9 7.7 %collective-permute-start.1 = (bf16[2,16,16,256]{3,2,1,0:T(8,128)(2,1)S(1)}, bf16[2,16,16,256]{3,2,1,0:T(8,128)(2,1)S(1)}, u32[]{:S(2)}, u32[]{:S(2)}) collective-permute-start(bf16[2,16,16,256]{3,2,1,0:T(8,128)(2,1)S(1)} %get-tuple-element.89), channel_id=1, source_target_pairs={{1,0},{2,1},{3,2},{4,3},{5,4},{6,5},{7,6},{8,7},{9,8},{10,9},{11,1... | collective-permute-start | bytes 786440 | tf_op jit(solution)/shard_map/ppermute | solution.py:23
  25.8 29.5 %copy-start.7 = (bf16[16,128,3,3]{1,0,3,2:T(8,128)(2,1)S(1)}, bf16[16,128,3,3]{1,0,3,2:T(8,128)(2,1)}, u32[]{:S(2)}) copy-start(bf16[16,128,3,3]{1,0,3,2:T(8,128)(2,1)} %param.30) | copy-start | bytes 110596
  25.8 29.5 %copy-start.8 = (f32[128]{0:T(128)S(1)}, f32[128]{0:T(128)}, u32[]{:S(2)}) copy-start(f32[128]{0:T(128)} %param.29) | copy-start | bytes 1540
  49.6 5.7 %copy-start.9 = (f32[8,128,16,256]{1,0,3,2:T(8,128)}, f32[8,128,16,256]{1,0,3,2:T(8,128)S(1)}, u32[]{:S(2)}) copy-start(f32[8,128,16,256]{1,0,3,2:T(8,128)S(1)} %fusion.22) | copy-start | bytes 50331652
  77.7 8.3 %copy-start.3 = (f32[8,16,256]{2,1,0:T(8,128)S(1)}, f32[8,16,256]{2,1,0:T(8,128)}, u32[]{:S(2)}) copy-start(f32[8,16,256]{2,1,0:T(8,128)} %param.24) | copy-start | bytes 393220
  77.7 8.3 %copy-start.6 = (f32[16]{0:T(128)S(1)}, f32[16]{0:T(128)}, u32[]{:S(2)}) copy-start(f32[16]{0:T(128)} %param.31) | copy-start | bytes 196
  148.3 4.6 %copy-start.1 = (f32[8,80,16,256]{3,2,1,0:T(8,128)S(1)}, f32[8,80,16,256]{3,2,1,0:T(8,128)}, u32[]{:S(2)}) copy-start(f32[8,80,16,256]{3,2,1,0:T(8,128)} %copy.54) | copy-start | bytes 31457284
  154.9 7.7 %collective-permute-start.2 = (bf16[2,16,16,256]{3,2,1,0:T(8,128)(2,1)S(1)}, bf16[2,16,16,256]{3,2,1,0:T(8,128)(2,1)S(1)}, u32[]{:S(2)}, u32[]{:S(2)}) collective-permute-start(bf16[2,16,16,256]{3,2,1,0:T(8,128)(2,1)S(1)} %slice.338), channel_id=1, source_target_pairs={{1,0},{2,1},{3,2},{4,3},{5,4},{6,5},{7,6},{8,7},{9,8},{10,9},{11,1... | collective-permute-start | bytes 786440 | tf_op jit(solution)/shard_map/ppermute | solution.py:31
  156.9 9.7 %collective-permute-start.3 = (bf16[2,16,16,256]{3,2,1,0:T(8,128)(2,1)S(1)}, bf16[2,16,16,256]{3,2,1,0:T(8,128)(2,1)S(1)}, u32[]{:S(2)}, u32[]{:S(2)}) collective-permute-start(bf16[2,16,16,256]{3,2,1,0:T(8,128)(2,1)S(1)} %slice.337), channel_id=1, source_target_pairs={{0,1},{1,2},{2,3},{3,4},{4,5},{5,6},{6,7},{7,8},{8,9},{9,10},{10,1... | collective-permute-start | bytes 786440 | tf_op jit(solution)/shard_map/ppermute | solution.py:31
  160.6 6.1 %copy-start.4 = (s32[8,16,256]{2,1,0:T(8,128)S(1)}, s32[8,16,256]{2,1,0:T(8,128)}, u32[]{:S(2)}) copy-start(s32[8,16,256]{2,1,0:T(8,128)} %param.26) | copy-start | bytes 393220
where the time goes:
time: 172 us; the launch traced here: 169 us
  matrix products  84.9 us (49%)
  local copies, waits for them, and re-layouts  46.8 us (27%)
  other arithmetic  16.2 us (9%)
  starting transfers between devices  12.1 us (7%)
  waiting for transfers between devices  8.02 us (5%)
    conv_general_dilated x4, matrix products, conv(): lax.conv_general_dilated(value, kernel, (1, 1), ((1, 1), (1, 1)), dimensi...  84.9 us
    conv_general_dilated x2, local copies, waits for them, and re-layouts, conv(): lax.conv_general_dilated(value, kernel, (1, 1), ((1, 1), (1, 1)), dimensi...  20 us
    concatenate x1, local copies, waits for them, and re-layouts, stack_windows(): return jnp.concatenate([source[k:k + frames] for k in range(span)], axis=1)  8.99 us
    unnamed x20, local copies, waits for them, and re-layouts  7.68 us
    convert_element_type x1, local copies, waits for them, and re-layouts, per_device(): misfit_b = misfit.astype(jnp.bfloat16)  7.46 us
    ppermute x2, waiting for transfers between devices, passed_along(): lax.ppermute(value, axis, [(source, source + steps) for source in range(i...  5.72 us
    ppermute x2, starting transfers between devices, passed_along(): lax.ppermute(value, axis, [(source, source + steps) for source in range(i...  5.56 us
    ppermute x1, starting transfers between devices, with_halo(): before = lax.ppermute(last, axis, up)  4.64 us
  transfers between devices with their start and end apart: 4, of which 4 were waited for; matrix products, arithmetic and copies ran while one was open for 2% of the time, Pallas kernels for 0%

commit v1 on v0

v1 whole, which is shorter than its diff:
```python
import functools

import jax
import jax.numpy as jnp
from jax import lax
from jax.experimental import pallas as pl
from jax.experimental.pallas import tpu as pltpu
from jax.sharding import PartitionSpec as P

STEPS = 64
ROWS = 16
COLS = 256


sigma_low = 0.1
sigma_ratio = 20.0


def with_halo(x, sides, width):
    for axis, dim in sides:
        peers, length = (lax.axis_size(axis), x.shape[dim])
        up = [(i, (i + 1) % peers) for i in range(peers - 1)]
        down = [(j, i) for i, j in up]
        last = lax.slice_in_dim(x, length - width, length, axis=dim)
        initial = lax.slice_in_dim(x, 0, width, axis=dim)
        before = lax.ppermute(last, axis, up)
        after = lax.ppermute(initial, axis, down)
        x = jnp.concatenate([before, x, after], axis=dim)
    return x


def passed_along(value, axis, steps):
    count = lax.axis_size(axis)
    initial, last = (max(0, -steps), min(count, count - steps))
    return lax.ppermute(value, axis, [(source, source + steps) for source in range(initial, last)])


def frame_kernel(
    sc_ref, ext_ref, noisy_ref, obs_ref, mask_ref, chan_ref,
    w1_ref, b1_ref, w2z_ref, b2_ref, w2t_ref, w1t_ref,
    a_ref, back_ref,
):
    f32, bf16 = jnp.float32, jnp.bfloat16
    t = pl.program_id(0)
    chans = noisy_ref.shape[1]
    pix = noisy_ref.shape[2]
    span = w1_ref.shape[2] // (3 * chans)

    @pl.when(t == 0)
    def _():
        back_ref[...] = jnp.zeros_like(back_ref)

    lane = lax.broadcasted_iota(jnp.int32, (1, pix), 1)
    col = lane % COLS

    def shift_x(v, d):
        if d == 0:
            return v
        r = pltpu.roll(v, (-d) % pix, 1)
        ok = (col + d >= 0) & (col + d < COLS)
        return jnp.where(ok, r, jnp.zeros_like(r))

    def shift_y(v, d):
        if d == 0:
            return v
        z = jnp.zeros((v.shape[0], COLS * abs(d)), v.dtype)
        if d > 0:
            return jnp.concatenate([v[:, d * COLS :], z], axis=1)
        return jnp.concatenate([z, v[:, : d * COLS]], axis=1)

    win = jnp.concatenate([ext_ref[t + k] for k in range(span)], axis=0).astype(f32)
    xcat = jnp.concatenate([shift_x(win, b - 1).astype(bf16) for b in range(3)], axis=0)
    pre = None
    for a in range(3):
        d = jnp.dot(w1_ref[a], shift_y(xcat, a - 1), preferred_element_type=f32)
        pre = d if pre is None else pre + d
    pre = pre + b1_ref[...]
    sig = 1.0 / (1.0 + jnp.exp(-pre))
    hidden = (pre * sig).astype(bf16)
    deriv = sig * (1.0 + pre * (1.0 - sig))

    z = jnp.dot(w2z_ref[...], hidden, preferred_element_type=f32)
    conv2 = None
    for b in range(3):
        s = None
        for a in range(3):
            r0 = (a * 3 + b) * chans
            v = shift_y(z[r0 : r0 + chans], a - 1)
            s = v if s is None else s + v
        s = shift_x(s, b - 1)
        conv2 = s if conv2 is None else conv2 + s
    den = noisy_ref[0].astype(f32) + conv2 + b2_ref[...]

    cid = lax.broadcasted_iota(jnp.int32, (chans, pix), 0)
    sel = (chan_ref[0] == cid) & (mask_ref[0] == 1)
    misfit = jnp.where(sel, den - obs_ref[0], 0.0)
    a_ref[0] = den - sc_ref[1] * misfit

    mb = misfit.astype(bf16).astype(f32)
    g = jnp.concatenate(
        [shift_x(shift_y(mb, 1 - a), 1 - b).astype(bf16) for a in range(3) for b in range(3)],
        axis=0,
    )
    ghp = jnp.dot(w2t_ref[...], g, preferred_element_type=f32)
    gh = (ghp * deriv).astype(bf16).astype(f32)

    hcat = jnp.concatenate([shift_x(gh, 1 - b).astype(bf16) for b in range(3)], axis=0)
    gw = None
    for a in range(3):
        d = jnp.dot(w1t_ref[a], shift_y(hcat, 1 - a), preferred_element_type=f32)
        gw = d if gw is None else gw + d
    for k in range(span):
        back_ref[t + k] += gw[k * chans : (k + 1) * chans]


def per_device(
    noisy, observed, obs_mask, obs_channel, step_index, w_first, b_first, w_second, b_second
):
    frames = noisy.shape[0]
    chans = noisy.shape[1]
    hid = w_first.shape[0]
    span = w_first.shape[1] // chans
    half = span // 2
    pix = ROWS * COLS
    level = step_index[0].astype(jnp.float32) / jnp.float32(STEPS - 1)
    sigma = jnp.float32(sigma_low) * jnp.exp(jnp.log(jnp.float32(sigma_ratio)) * level)
    c_in = 1.0 / jnp.sqrt(1.0 + sigma * sigma)
    weight_obs = 1.0 / (1.0 + sigma * sigma)
    scaled = (c_in * noisy.astype(jnp.float32)).astype(jnp.bfloat16)
    extended = with_halo(scaled, (("tm", 0),), half).reshape(frames + 2 * half, chans, pix)

    w1 = jnp.transpose(w_first, (2, 0, 3, 1)).reshape(3, hid, 3 * span * chans)
    w1t = jnp.transpose(w_first, (2, 1, 3, 0)).reshape(3, span * chans, 3 * hid)
    w2z = jnp.transpose(w_second, (2, 3, 0, 1)).reshape(9 * chans, hid)
    w2t = jnp.transpose(w_second, (1, 2, 3, 0)).reshape(hid, 9 * chans)
    sc = jnp.stack([c_in, weight_obs]).astype(jnp.float32)

    full = lambda shape: pl.BlockSpec(shape, lambda t: (0,) * len(shape))
    frame = lambda shape: pl.BlockSpec(shape, lambda t: (t,) + (0,) * (len(shape) - 1))
    a_part, back_pad = pl.pallas_call(
        frame_kernel,
        grid=(frames,),
        in_specs=[
            pl.BlockSpec(memory_space=pltpu.SMEM),
            full((frames + 2 * half, chans, pix)),
            frame((1, chans, pix)),
            frame((1, 1, pix)),
            frame((1, 1, pix)),
            frame((1, 1, pix)),
            full(w1.shape),
            full((hid, 1)),
            full(w2z.shape),
            full((chans, 1)),
            full(w2t.shape),
            full(w1t.shape),
        ],
        out_specs=[
            frame((1, chans, pix)),
            full((frames + 2 * half, chans, pix)),
        ],
        out_shape=[
            jax.ShapeDtypeStruct((frames, chans, pix), jnp.float32),
            jax.ShapeDtypeStruct((frames + 2 * half, chans, pix), jnp.float32),
        ],
        compiler_params=pltpu.CompilerParams(dimension_semantics=("arbitrary",)),
    )(
        sc,
        extended,
        noisy.reshape(frames, chans, pix),
        observed.reshape(frames, 1, pix),
        obs_mask.reshape(frames, 1, pix),
        obs_channel.reshape(frames, 1, pix),
        w1,
        b_first.reshape(hid, 1),
        w2z,
        b_second.reshape(chans, 1),
        w2t,
        w1t,
    )
    from_right = passed_along(back_pad[:half].astype(jnp.bfloat16), "tm", -1).astype(jnp.float32)
    from_left = passed_along(back_pad[frames + half :].astype(jnp.bfloat16), "tm", 1).astype(
        jnp.float32
    )
    back = back_pad[half : frames + half]
    back = back.at[frames - half :].add(from_right)
    back = back.at[:half].add(from_left)
    guided = a_part - (weight_obs * c_in) * back
    return guided.reshape(noisy.shape)


def solution(mesh):
    return jax.shard_map(
        per_device,
        mesh=mesh,
        in_specs=(
            P(("groups", "tm"), None, None, None),
            P(("groups", "tm"), None, None),
            P(("groups", "tm"), None, None),
            P(("groups", "tm"), None, None),
            P("groups"),
            P(),
            P(),
            P(),
            P(),
        ),
        out_specs=P(("groups", "tm"), None, None, None),
        check_vma=False,
    )
```

time: 172 us -> 83.6 us (0.49); the launches traced: 169 us -> 82.7 us
  matrix products: 84.9 us -> 0 us
  Pallas kernels: 0 us -> 44.3 us
  local copies, waits for them, and re-layouts: 46.8 us -> 16 us
  other arithmetic: 16.2 us -> 4.87 us
  waiting for transfers between devices: 8.02 us -> 4.4 us
    conv_general_dilated x4 -> x0, matrix products: 84.9 us -> none  [conv(): lax.conv_general_dilated(value, kernel, (1, 1), ((1, 1), (1, 1)), dimensi...]
    pallas_call x0 -> x1, Pallas kernels: none -> 44.3 us  [per_device(): pl.pallas_call(frame_kernel, grid=(frames,), in_specs=[pl.BlockSpec(memor...]
    conv_general_dilated x2 -> x0, local copies, waits for them, and re-layouts: 20 us -> none  [conv(): lax.conv_general_dilated(value, kernel, (1, 1), ((1, 1), (1, 1)), dimensi...]
    reshape x0 -> x10, local copies, waits for them, and re-layouts: none -> 12.2 us  [the longest x1 2.11 us: per_device(): with_halo(scaled, (('tm', 0),), half).reshape(frames + 2 * half, chans, pix)]
    concatenate x1 -> x0, local copies, waits for them, and re-layouts: 8.99 us -> none  [stack_windows(): return jnp.concatenate([source[k:k + frames] for k in range(span)], axis=1)]
    convert_element_type x1 -> x0, local copies, waits for them, and re-layouts: 7.46 us -> none  [per_device(): misfit_b = misfit.astype(jnp.bfloat16)]
    unnamed x20 -> x17, local copies, waits for them, and re-layouts: 7.68 us -> 2.81 us
    unnamed x4 -> x0, other arithmetic: 4.49 us -> none
  transfers between devices with their start and end apart: 4 -> 4, of which waited for: 4 -> 2; matrix products, arithmetic and copies ran while one was open for 2% -> 13% of each run, Pallas kernels for 0% -> 0%
where the time goes in v1:
time: 83.6 us; the launch traced here: 82.7 us
  Pallas kernels  44.3 us (53%)
  local copies, waits for them, and re-layouts  16 us (19%)
  starting transfers between devices  12.1 us (14%)
  other arithmetic  4.87 us (6%)
  waiting for transfers between devices  4.4 us (5%)
  between operations  1.04 us (1%)
    pallas_call x1, Pallas kernels, per_device(): pl.pallas_call(frame_kernel, grid=(frames,), in_specs=[pl.BlockSpec(memor...  44.3 us
    ppermute x2, starting transfers between devices, passed_along(): lax.ppermute(value, axis, [(source, source + steps) for source in range(i...  5.54 us
    ppermute x1, starting transfers between devices, with_halo(): before = lax.ppermute(last, axis, up)  4.64 us
    ppermute x2, waiting for transfers between devices, passed_along(): lax.ppermute(value, axis, [(source, source + steps) for source in range(i...  4.39 us
    unnamed x17, local copies, waits for them, and re-layouts  2.81 us
    another operation x1, other arithmetic  2.23 us
    reshape x1, local copies, waits for them, and re-layouts, per_device(): with_halo(scaled, (('tm', 0),), half).reshape(frames + 2 * half, chans, pix)  2.11 us
    ppermute x1, starting transfers between devices, with_halo(): after = lax.ppermute(initial, axis, down)  1.92 us
  transfers between devices with their start and end apart: 4, of which 2 were waited for; matrix products, arithmetic and copies ran while one was open for 13% of the time, Pallas kernels for 0%

profile of v1, /device:TPU:1, one launch (start us, length us, event | category | flops | bytes accessed | tf_op | source)
XLA Modules:
  0.0 82.7 jit_solution(40225107715815763)
XLA Ops:
  0.8 1.4 %multiply_convert_fusion = bf16[8,16,16,256]{3,2,1,0:T(8,128)(2,1)S(1)} fusion(bf16[8,16,16,256]{3,2,1,0:T(8,128)(2,1)} %param.13, f32[]{:T(128)} %bitcast), kind=kLoop, calls=%fused_computation.1 | loop fusion | flops 1572864 | bytes 2097156 | tf_op jit(solution)/shard_map/convert_element_type | solution.py:129
  2.3 4.6 %collective-permute-start = (bf16[2,16,16,256]{3,2,1,0:T(8,128)(2,1)S(1)}, bf16[2,16,16,256]{3,2,1,0:T(8,128)(2,1)S(1)}, u32[]{:S(2)}, u32[]{:S(2)}) collective-permute-start(bf16[2,16,16,256]{3,2,1,0:T(8,128)(2,1)S(1)} %get-tuple-element.35), channel_id=1, source_target_pairs={{0,1},{1,2},{2,3},{3,4},{4,5},{5,6},{6,7},{7,8},{8,9},{9,10},{10,1... | collective-permute-start | bytes 786440 | tf_op jit(solution)/shard_map/ppermute | solution.py:26
  7.0 1.9 %collective-permute-start.1 = (bf16[2,16,16,256]{3,2,1,0:T(8,128)(2,1)S(1)}, bf16[2,16,16,256]{3,2,1,0:T(8,128)(2,1)S(1)}, u32[]{:S(2)}, u32[]{:S(2)}) collective-permute-start(bf16[2,16,16,256]{3,2,1,0:T(8,128)(2,1)S(1)} %get-tuple-element.36), channel_id=1, source_target_pairs={{1,0},{2,1},{3,2},{4,3},{5,4},{6,5},{7,6},{8,7},{9,8},{10,9},{11,1... | collective-permute-start | bytes 786440 | tf_op jit(solution)/shard_map/ppermute | solution.py:27
  9.0 0.6 pad_maximum_fusion.1.sc_ref
  9.6 1.3 %reshape.102.noisy_ref = bf16[8,16,4096]{2,1,0:T(8,128)(2,1)} reshape(bf16[8,16,16,256]{3,2,1,0:T(8,128)(2,1)S(1)} %copy-done.1) | data formatting | bytes 2097152 | tf_op jit(solution)/shard_map/reshape | solution.py:169
  10.9 0.7 copy.18.b2_ref
  11.6 0.7 copy.17.b1_ref
  12.3 0.7 copy.19.w2t_ref
  13.1 1.7 %reshape.103.obs_ref = f32[8,1,4096]{2,1,0:T(1,128)} reshape(f32[8,16,256]{2,1,0:T(8,128)} %param.14) | data formatting | bytes 262144 | tf_op jit(solution)/shard_map/reshape | solution.py:170
  14.8 1.7 %reshape.104.mask_ref = s32[8,1,4096]{2,1,0:T(1,128)} reshape(s32[8,16,256]{2,1,0:T(8,128)} %param.15) | data formatting | bytes 262144 | tf_op jit(solution)/shard_map/reshape | solution.py:171
  16.4 1.7 %reshape.105.chan_ref = s32[8,1,4096]{2,1,0:T(1,128)} reshape(s32[8,16,256]{2,1,0:T(8,128)} %param.16) | data formatting | bytes 262144 | tf_op jit(solution)/shard_map/reshape | solution.py:172
  18.1 0.8 %copy.16.w1_ref = bf16[3,128,240]{2,1,0:T(8,128)(2,1)} copy(bf16[3,128,240]{1,2,0:T(8,128)(2,1)S(1)} %bitcast.28) | data formatting | bytes 368640 | tf_op jit(solution)/shard_map/reshape | solution.py:132
  19.0 0.7 copy_bitcast_fusion.w1t_ref
  19.9 2.1 %reshape.101.ext_ref = bf16[12,16,4096]{2,1,0:T(8,128)(2,1)} reshape(bf16[12,16,16,256]{3,2,1,0:T(8,128)(2,1)S(1)} %pad_maximum_fusion) | data formatting | bytes 3145728 | tf_op jit(solution)/shard_map/reshape | solution.py:130
  22.0 44.3 %shard_map.91 = (f32[8,16,4096]{2,1,0:T(8,128)}, f32[12,16,4096]{2,1,0:T(8,128)}) custom-call(f32[2]{0:T(128)} %pad_maximum_fusion.1.sc_ref, bf16[12,16,4096]{2,1,0:T(8,128)(2,1)} %reshape.101.ext_ref, bf16[8,16,4096]{2,1,0:T(8,128)(2,1)} %reshape.102.noisy_ref, f32[8,1,4096]{2,1,0:T(1,128)} %reshape.103.obs_ref, s32[8,1,4096]{2,1,0:T(1,128)} %reshape.104.mask_ref, ...), custom_call_target="tpu_custom_call" | custom-call | tf_op jit(solution)/shard_map/pallas_call | solution.py:140
  66.3 2.2 %convert.4 = bf16[12,16,4096]{2,1,0:T(8,128)(2,1)S(1)} convert(f32[12,16,4096]{2,1,0:T(8,128)} %get-tuple-element.32) | non-fusion elementwise | flops 786432 | bytes 4718592 | tf_op jit(solution)/shard_map/convert.1
  68.5 0.8 %fusion.1 = (bf16[2,16,4096]{2,1,0:T(8,128)(2,1)}, bf16[2,16,4096]{2,1,0:T(8,128)(2,1)}) fusion(bf16[12,16,4096]{2,1,0:T(8,128)(2,1)S(1)} %convert.4), kind=kLoop, calls=%fused_computation.8 | loop fusion | bytes 1048576 | tf_op jit(solution)/shard_map/slice | solution.py:181
  69.4 1.9 %collective-permute-start.2 = (bf16[2,16,4096]{2,1,0:T(8,128)(2,1)}, bf16[2,16,4096]{2,1,0:T(8,128)(2,1)S(1)}, u32[]{:S(2)}, u32[]{:S(2)}) collective-permute-start(bf16[2,16,4096]{2,1,0:T(8,128)(2,1)} %get-tuple-element.34), channel_id=1, source_target_pairs={{1,0},{2,1},{3,2},{4,3},{5,4},{6,5},{7,6},{8,7},{9,8},{10,9},{11,1... | collective-permute-start | bytes 786440 | tf_op jit(solution)/shard_map/ppermute | solution.py:35
  71.5 0.8 copy-done.4
  72.2 3.6 %collective-permute-start.3 = (bf16[2,16,4096]{2,1,0:T(8,128)(2,1)S(1)}, bf16[2,16,4096]{2,1,0:T(8,128)(2,1)S(1)}, u32[]{:S(2)}, u32[]{:S(2)}) collective-permute-start(bf16[2,16,4096]{2,1,0:T(8,128)(2,1)S(1)} %copy-done.4), channel_id=1, source_target_pairs={{0,1},{1,2},{2,3},{3,4},{4,5},{5,6},{6,7},{7,8},{8,9},{9,10},{10,1... | collective-permute-start | bytes 786440 | tf_op jit(solution)/shard_map/ppermute | solution.py:35
  75.9 1.4 %collective-permute-done.2 = bf16[2,16,4096]{2,1,0:T(8,128)(2,1)S(1)} collective-permute-done((bf16[2,16,4096]{2,1,0:T(8,128)(2,1)}, bf16[2,16,4096]{2,1,0:T(8,128)(2,1)S(1)}, u32[]{:S(2)}, u32[]{:S(2)}) %collective-permute-start.2) | collective-permute-done | bytes 262176 | tf_op jit(solution)/shard_map/ppermute | solution.py:35
  77.3 3.0 %collective-permute-done.3 = bf16[2,16,4096]{2,1,0:T(8,128)(2,1)S(1)} collective-permute-done((bf16[2,16,4096]{2,1,0:T(8,128)(2,1)S(1)}, bf16[2,16,4096]{2,1,0:T(8,128)(2,1)S(1)}, u32[]{:S(2)}, u32[]{:S(2)}) %collective-permute-start.3) | collective-permute-done | bytes 262176 | tf_op jit(solution)/shard_map/ppermute | solution.py:35
  80.4 0.3 multiply_subtract_fusion
  80.7 2.0 %copy.21 = f32[16,8,16,256]{3,2,1,0:T(8,128)} copy(f32[16,8,16,256]{3,1,2,0:T(8,128)S(1)} %bitcast.27) | data formatting | bytes 4194304
  (22 shorter events, 0.6 us)
Async XLA Ops:
  0.0 9.6 %copy-start.1 = (bf16[8,16,16,256]{3,2,1,0:T(8,128)(2,1)S(1)}, bf16[8,16,16,256]{3,2,1,0:T(8,128)(2,1)}, u32[]{:S(2)}) copy-start(bf16[8,16,16,256]{3,2,1,0:T(8,128)(2,1)} %param.13) | copy-start | bytes 3145732
  2.3 8.7 %copy-start.7 = (f32[16]{0:T(128)S(1)}, f32[16]{0:T(128)}, u32[]{:S(2)}) copy-start(f32[16]{0:T(128)} %param.21) | copy-start | bytes 196
  2.3 9.3 %copy-start.6 = (f32[128]{0:T(128)S(1)}, f32[128]{0:T(128)}, u32[]{:S(2)}) copy-start(f32[128]{0:T(128)} %param.19) | copy-start | bytes 1540
  2.3 10.0 %copy-start.5 = (bf16[16,128,3,3]{1,0,3,2:T(8,128)(2,1)S(1)}, bf16[16,128,3,3]{1,0,3,2:T(8,128)(2,1)}, u32[]{:S(2)}) copy-start(bf16[16,128,3,3]{1,0,3,2:T(8,128)(2,1)} %param.20) | copy-start | bytes 110596
  2.3 15.8 %copy-start.3 = (bf16[128,80,3,3]{0,1,3,2:T(8,128)(2,1)S(1)}, bf16[128,80,3,3]{0,1,3,2:T(8,128)(2,1)}, u32[]{:S(2)}) copy-start(bf16[128,80,3,3]{0,1,3,2:T(8,128)(2,1)} %param.18) | copy-start | bytes 552964
  2.3 17.3 %collective-permute-start = (bf16[2,16,16,256]{3,2,1,0:T(8,128)(2,1)S(1)}, bf16[2,16,16,256]{3,2,1,0:T(8,128)(2,1)S(1)}, u32[]{:S(2)}, u32[]{:S(2)}) collective-permute-start(bf16[2,16,16,256]{3,2,1,0:T(8,128)(2,1)S(1)} %get-tuple-element.35), channel_id=1, source_target_pairs={{0,1},{1,2},{2,3},{3,4},{4,5},{5,6},{6,7},{7,8},{8,9},{9,10},{10,1... | collective-permute-start | bytes 786440 | tf_op jit(solution)/shard_map/ppermute | solution.py:26
  7.0 12.7 %collective-permute-start.1 = (bf16[2,16,16,256]{3,2,1,0:T(8,128)(2,1)S(1)}, bf16[2,16,16,256]{3,2,1,0:T(8,128)(2,1)S(1)}, u32[]{:S(2)}, u32[]{:S(2)}) collective-permute-start(bf16[2,16,16,256]{3,2,1,0:T(8,128)(2,1)S(1)} %get-tuple-element.36), channel_id=1, source_target_pairs={{1,0},{2,1},{3,2},{4,3},{5,4},{6,5},{7,6},{8,7},{9,8},{10,9},{11,1... | collective-permute-start | bytes 786440 | tf_op jit(solution)/shard_map/ppermute | solution.py:27
  66.3 5.0 %copy-start = (f32[12,16,4096]{2,1,0:T(8,128)S(1)}, f32[12,16,4096]{2,1,0:T(8,128)}, u32[]{:S(2)}) copy-start(f32[12,16,4096]{2,1,0:T(8,128)} %get-tuple-element.32) | copy-start | bytes 9437188
  69.4 7.9 %collective-permute-start.2 = (bf16[2,16,4096]{2,1,0:T(8,128)(2,1)}, bf16[2,16,4096]{2,1,0:T(8,128)(2,1)S(1)}, u32[]{:S(2)}, u32[]{:S(2)}) collective-permute-start(bf16[2,16,4096]{2,1,0:T(8,128)(2,1)} %get-tuple-element.34), channel_id=1, source_target_pairs={{1,0},{2,1},{3,2},{4,3},{5,4},{6,5},{7,6},{8,7},{9,8},{10,9},{11,1... | collective-permute-start | bytes 786440 | tf_op jit(solution)/shard_map/ppermute | solution.py:35
  71.3 1.0 %copy-start.4 = (bf16[2,16,4096]{2,1,0:T(8,128)(2,1)S(1)}, bf16[2,16,4096]{2,1,0:T(8,128)(2,1)}, u32[]{:S(2)}) copy-start(bf16[2,16,4096]{2,1,0:T(8,128)(2,1)} %get-tuple-element.33) | copy-start | bytes 786436
  71.4 9.0 %copy-start.2 = (f32[8,16,4096]{2,1,0:T(8,128)S(1)}, f32[8,16,4096]{2,1,0:T(8,128)}, u32[]{:S(2)}) copy-start(f32[8,16,4096]{2,1,0:T(8,128)} %get-tuple-element.31) | copy-start | bytes 6291460
  72.2 8.1 %collective-permute-start.3 = (bf16[2,16,4096]{2,1,0:T(8,128)(2,1)S(1)}, bf16[2,16,4096]{2,1,0:T(8,128)(2,1)S(1)}, u32[]{:S(2)}, u32[]{:S(2)}) collective-permute-start(bf16[2,16,4096]{2,1,0:T(8,128)(2,1)S(1)} %copy-done.4), channel_id=1, source_target_pairs={{0,1},{1,2},{2,3},{3,4},{4,5},{5,6},{6,7},{7,8},{8,9},{9,10},{10,1... | collective-permute-start | bytes 786440 | tf_op jit(solution)/shard_map/ppermute | solution.py:35
